TPU v7x, 256 devices: a whole 4x4x8 slice. The times are simulated.
256 devices in a mesh: dp: 16 (over x, y_lo, core), expert: 16 (over z, y_hi).
Axes of the slice: x: 4, y: 4 (y_hi: 2, y_lo: 2; y = y_hi * 2 + y_lo), z: 8, core: 2. Of those that a mesh axis runs over, the one named last changes fastest.
Arguments:
- tokens: bfloat16 [32768, 2048], P(('dp', 'expert')), may hold values from -6 to 6
- gain: float32 [2048], replicated, may hold values from 0.1 to 1.9
- expert_ids: int32 [32768, 8], P(('dp', 'expert')), may hold values from 0 to 15, all different within a row; in each aligned block of 128 rows (0 to 127, 128 to 255, ...) at most 96 rows name the same one
- gate_values: float32 [32768, 8], P(('dp', 'expert')), may hold values from 0.02 to 0.25
- w_gate: bfloat16 [16, 2048, 768], P('expert'), may hold values from -0.125 to 0.125
- w_up: bfloat16 [16, 2048, 768], P('expert'), may hold values from -0.125 to 0.125
- w_down: bfloat16 [16, 768, 2048], P('expert'), may hold values from -0.21875 to 0.21875
Outputs:
- mixed: bfloat16 [32768, 2048], P(('dp', 'expert'))
Inputs may be any that keep to these rules, and one draw needn't show every extreme that they name: `expert_ids`: each row names 8 different experts. In the rows of one device no expert is named by more than 96 rows, and in every draw some expert is named by exactly 96 rows of some device.
All inputs are finite; a program needn't handle non-finite values.
Results may differ from a plain program's by a relative error of at most 0.018.
Values may be sent and summed in bfloat16 or wider, within the bound.
No kernel may reach another device: no remote copies, remote signals or barrier semaphores. Data moves between devices by JAX's collectives and lax.ppermute only.
A program may use at most 128 MiB of HBM per device.

v0:
```python
import jax
import jax.numpy as jnp
from jax import lax
from jax.sharding import PartitionSpec as P

eps_value = 1e-06


def passed_along(block, axis, distance):
    devices = range(lax.axis_size(axis))
    route = [((i - distance) % len(devices), i) for i in devices]
    return lax.ppermute(block, axis, route)


def normalize(tokens, gain):
    values = tokens.astype(jnp.float32)
    meansq = jnp.mean(values * values, axis=-1, keepdims=True)
    return (values * lax.rsqrt(meansq + eps_value) * gain).astype(jnp.bfloat16)


def gate_dense(expert_ids, gate_values, number):
    labels = jnp.arange(number, dtype=jnp.int32)
    hits = (expert_ids[..., None] == labels).astype(jnp.float32)
    return jnp.sum(hits * gate_values[..., None], axis=-2)


def dispatch_table(column, capacity):
    matched = (column > 0).astype(jnp.float32)
    slots = jnp.cumsum(matched, axis=-1) - 1.0
    places = jnp.arange(capacity).astype(jnp.float32)
    chosen = (slots[..., None, :] == places[:, None]) & (matched[..., None, :] > 0)
    return chosen.astype(jnp.bfloat16)


def expert_mlp(slot_rows, gate_matrix, up_matrix, down_matrix):
    gated = jnp.dot(slot_rows, gate_matrix, preferred_element_type=jnp.float32)
    upward = jnp.dot(slot_rows, up_matrix, preferred_element_type=jnp.float32)
    hidden = (jax.nn.silu(gated) * upward).astype(jnp.bfloat16)
    return jnp.dot(hidden, down_matrix, preferred_element_type=jnp.float32).astype(jnp.bfloat16)


def place_block(buffer, table, carried, source):
    picked = lax.dynamic_index_in_dim(table, source, 0, keepdims=False)
    slot_rows = jnp.dot(picked, carried, preferred_element_type=jnp.float32).astype(jnp.bfloat16)
    return lax.dynamic_update_index_in_dim(buffer, slot_rows, source, 0)


def local(tokens, gain, expert_ids, gate_values, w_gate, w_up, w_down):
    group = lax.axis_size("expert")
    position = lax.axis_index("expert")
    local_rows = tokens.shape[0]
    width = tokens.shape[1]
    chosen_count = expert_ids.shape[1]
    capacity = local_rows * chosen_count // group * 3 // 2
    gate_matrix = w_gate[0]
    up_matrix = w_up[0]
    down_matrix = w_down[0]
    normed = normalize(tokens, gain)
    dense = gate_dense(expert_ids, gate_values, group)
    gathered = lax.all_gather(dense, "expert", axis=0, tiled=True)
    column = lax.dynamic_slice_in_dim(gathered, position, 1, 1).reshape(group, local_rows)
    table = dispatch_table(column, capacity)
    buffer = jnp.zeros((group, capacity, width), jnp.bfloat16)
    buffer = place_block(buffer, table, normed, position)

    def forward_turn(offset, state):
        current, carried = state
        carried = passed_along(carried, "expert", 1)
        source = (position - offset) % group
        return (place_block(current, table, carried, source), carried)

    buffer, carried = lax.fori_loop(1, group, forward_turn, (buffer, normed))
    outputs = expert_mlp(
        buffer.reshape(group * capacity, width), gate_matrix, up_matrix, down_matrix
    )
    outputs = outputs.reshape(group, capacity, width)
    spanned = local_rows * lax.axis_size("expert") // local_rows
    back = jnp.einsum("bct,bcd->btd", table, outputs, preferred_element_type=jnp.float32)
    return lax.psum_scatter(
        (back * column[:, :, None]).reshape(spanned * local_rows, width).astype(jnp.bfloat16),
        "expert",
        scatter_dimension=0,
        tiled=True,
    )


def solution(mesh):
    return jax.shard_map(
        local,
        mesh=mesh,
        in_specs=(
            P(("dp", "expert"), None),
            P(),
            P(("dp", "expert"), None),
            P(("dp", "expert"), None),
            P("expert", None, None),
            P("expert", None, None),
            P("expert", None, None),
        ),
        out_specs=P(("dp", "expert"), None),
        check_vma=False,
    )
```

profile of v0, /device:TPU:2, one launch (start us, length us, event | category | flops | bytes accessed | tf_op | source)
XLA Modules:
  0.0 603.0 jit_solution(9800306333503433712)
XLA Ops:
  6.5 0.5 iota_convert_fusion
  7.0 1.5 fusion.11
  8.5 0.7 select_reduce_fusion
  9.3 44.7 %all_gather.3 = f32[2048,16]{0,1:T(8,128)S(1)} all-gather(f32[128,16]{0,1:T(8,128)S(1)} %select_reduce_fusion), channel_id=1, replica_groups=mesh['dp'=16,'expert'=16] {'expert'}, dimensions={0}, use_global_device_ids=true | all-gather | bytes 139264 | tf_op jit(solution)/shard_map/all_gather | solution.py:60
  54.0 0.6 broadcast_compare_fusion
  54.6 0.3 reduce_window_sum.11
  54.9 1.2 fusion.13
  56.1 0.0 copy-start.3
  56.2 0.9 fusion.17
  57.1 0.8 broadcast_in_dim.24
  57.9 0.3 fusion.10
  58.2 2.6 copy-done.1
  60.8 287.0 %while.17 = (s32[]{:T(128)}, bf16[16,96,2048]{2,1,0:T(8,128)(2,1)}, bf16[128,2048]{1,0:T(8,128)(2,1)}, s32[]{:T(128)}, bf16[16,96,128]{2,1,0:T(8,128)(2,1)S(1)},...) while((s32[]{:T(128)}, bf16[16,96,2048]{2,1,0:T(8,128)(2,1)}, bf16[128,2048]{1,0:T(8,128)(2,1)}, s32[]{:T(128)}, ...), condition=%wide.region_4.5_spmd, body=%wide.region_3.4_spmd.sunk | while | flops 50528272 | bytes 4089120 | solution.py:72
  60.8 13.1 %collective-permute-done = bf16[128,2048]{1,0:T(8,128)(2,1)} collective-permute-done((bf16[128,2048]{1,0:T(8,128)(2,1)}, bf16[128,2048]{1,0:T(8,128)(2,1)}, u32[]{:S(2)}, u32[]{:S(2)}) %collective-permute-start) | collective-permute-done | bytes 524320 | tf_op jit(solution)/shard_map/while/body/eval_jaxpr/ppermute | solution.py:12
  73.9 1.9 copy.20
  75.8 2.1 fusion.29
  77.8 13.1 %collective-permute-done = bf16[128,2048]{1,0:T(8,128)(2,1)} collective-permute-done((bf16[128,2048]{1,0:T(8,128)(2,1)}, bf16[128,2048]{1,0:T(8,128)(2,1)}, u32[]{:S(2)}, u32[]{:S(2)}) %collective-permute-start) | collective-permute-done | bytes 524320 | tf_op jit(solution)/shard_map/while/body/eval_jaxpr/ppermute | solution.py:12
  90.9 1.9 copy.20
  92.8 2.1 fusion.29
  94.9 13.5 %collective-permute-done = bf16[128,2048]{1,0:T(8,128)(2,1)} collective-permute-done((bf16[128,2048]{1,0:T(8,128)(2,1)}, bf16[128,2048]{1,0:T(8,128)(2,1)}, u32[]{:S(2)}, u32[]{:S(2)}) %collective-permute-start) | collective-permute-done | bytes 524320 | tf_op jit(solution)/shard_map/while/body/eval_jaxpr/ppermute | solution.py:12
  108.4 1.9 copy.20
  110.3 2.1 fusion.29
  112.4 14.6 %collective-permute-done = bf16[128,2048]{1,0:T(8,128)(2,1)} collective-permute-done((bf16[128,2048]{1,0:T(8,128)(2,1)}, bf16[128,2048]{1,0:T(8,128)(2,1)}, u32[]{:S(2)}, u32[]{:S(2)}) %collective-permute-start) | collective-permute-done | bytes 524320 | tf_op jit(solution)/shard_map/while/body/eval_jaxpr/ppermute | solution.py:12
  127.0 1.9 copy.20
  128.9 2.1 fusion.29
  131.0 15.8 %collective-permute-done = bf16[128,2048]{1,0:T(8,128)(2,1)} collective-permute-done((bf16[128,2048]{1,0:T(8,128)(2,1)}, bf16[128,2048]{1,0:T(8,128)(2,1)}, u32[]{:S(2)}, u32[]{:S(2)}) %collective-permute-start) | collective-permute-done | bytes 524320 | tf_op jit(solution)/shard_map/while/body/eval_jaxpr/ppermute | solution.py:12
  146.8 1.9 copy.20
  148.6 2.0 fusion.29
  150.7 16.9 %collective-permute-done = bf16[128,2048]{1,0:T(8,128)(2,1)} collective-permute-done((bf16[128,2048]{1,0:T(8,128)(2,1)}, bf16[128,2048]{1,0:T(8,128)(2,1)}, u32[]{:S(2)}, u32[]{:S(2)}) %collective-permute-start) | collective-permute-done | bytes 524320 | tf_op jit(solution)/shard_map/while/body/eval_jaxpr/ppermute | solution.py:12
  167.6 1.9 copy.20
  169.5 2.0 fusion.29
  171.6 18.1 %collective-permute-done = bf16[128,2048]{1,0:T(8,128)(2,1)} collective-permute-done((bf16[128,2048]{1,0:T(8,128)(2,1)}, bf16[128,2048]{1,0:T(8,128)(2,1)}, u32[]{:S(2)}, u32[]{:S(2)}) %collective-permute-start) | collective-permute-done | bytes 524320 | tf_op jit(solution)/shard_map/while/body/eval_jaxpr/ppermute | solution.py:12
  189.7 1.9 copy.20
  191.6 2.0 fusion.29
  193.6 18.2 %collective-permute-done = bf16[128,2048]{1,0:T(8,128)(2,1)} collective-permute-done((bf16[128,2048]{1,0:T(8,128)(2,1)}, bf16[128,2048]{1,0:T(8,128)(2,1)}, u32[]{:S(2)}, u32[]{:S(2)}) %collective-permute-start) | collective-permute-done | bytes 524320 | tf_op jit(solution)/shard_map/while/body/eval_jaxpr/ppermute | solution.py:12
  211.8 1.9 copy.20
  213.7 2.0 fusion.29
  215.7 17.4 %collective-permute-done = bf16[128,2048]{1,0:T(8,128)(2,1)} collective-permute-done((bf16[128,2048]{1,0:T(8,128)(2,1)}, bf16[128,2048]{1,0:T(8,128)(2,1)}, u32[]{:S(2)}, u32[]{:S(2)}) %collective-permute-start) | collective-permute-done | bytes 524320 | tf_op jit(solution)/shard_map/while/body/eval_jaxpr/ppermute | solution.py:12
  233.1 1.9 copy.20
  235.0 2.1 fusion.29
  237.0 16.5 %collective-permute-done = bf16[128,2048]{1,0:T(8,128)(2,1)} collective-permute-done((bf16[128,2048]{1,0:T(8,128)(2,1)}, bf16[128,2048]{1,0:T(8,128)(2,1)}, u32[]{:S(2)}, u32[]{:S(2)}) %collective-permute-start) | collective-permute-done | bytes 524320 | tf_op jit(solution)/shard_map/while/body/eval_jaxpr/ppermute | solution.py:12
  253.5 1.9 copy.20
  255.4 2.0 fusion.29
  257.4 15.7 %collective-permute-done = bf16[128,2048]{1,0:T(8,128)(2,1)} collective-permute-done((bf16[128,2048]{1,0:T(8,128)(2,1)}, bf16[128,2048]{1,0:T(8,128)(2,1)}, u32[]{:S(2)}, u32[]{:S(2)}) %collective-permute-start) | collective-permute-done | bytes 524320 | tf_op jit(solution)/shard_map/while/body/eval_jaxpr/ppermute | solution.py:12
  273.1 1.9 copy.20
  275.0 2.1 fusion.29
  277.1 14.8 %collective-permute-done = bf16[128,2048]{1,0:T(8,128)(2,1)} collective-permute-done((bf16[128,2048]{1,0:T(8,128)(2,1)}, bf16[128,2048]{1,0:T(8,128)(2,1)}, u32[]{:S(2)}, u32[]{:S(2)}) %collective-permute-start) | collective-permute-done | bytes 524320 | tf_op jit(solution)/shard_map/while/body/eval_jaxpr/ppermute | solution.py:12
  291.9 1.9 copy.20
  293.7 2.1 fusion.29
  295.8 13.9 %collective-permute-done = bf16[128,2048]{1,0:T(8,128)(2,1)} collective-permute-done((bf16[128,2048]{1,0:T(8,128)(2,1)}, bf16[128,2048]{1,0:T(8,128)(2,1)}, u32[]{:S(2)}, u32[]{:S(2)}) %collective-permute-start) | collective-permute-done | bytes 524320 | tf_op jit(solution)/shard_map/while/body/eval_jaxpr/ppermute | solution.py:12
  309.7 1.9 copy.20
  311.6 2.1 fusion.29
  313.7 13.1 %collective-permute-done = bf16[128,2048]{1,0:T(8,128)(2,1)} collective-permute-done((bf16[128,2048]{1,0:T(8,128)(2,1)}, bf16[128,2048]{1,0:T(8,128)(2,1)}, u32[]{:S(2)}, u32[]{:S(2)}) %collective-permute-start) | collective-permute-done | bytes 524320 | tf_op jit(solution)/shard_map/while/body/eval_jaxpr/ppermute | solution.py:12
  326.8 1.9 copy.20
  328.7 2.0 fusion.29
  330.7 13.1 %collective-permute-done = bf16[128,2048]{1,0:T(8,128)(2,1)} collective-permute-done((bf16[128,2048]{1,0:T(8,128)(2,1)}, bf16[128,2048]{1,0:T(8,128)(2,1)}, u32[]{:S(2)}, u32[]{:S(2)}) %collective-permute-start) | collective-permute-done | bytes 524320 | tf_op jit(solution)/shard_map/while/body/eval_jaxpr/ppermute | solution.py:12
  343.8 1.9 copy.20
  345.7 2.0 fusion.29
  347.8 8.2 %fusion.7 = f32[1536,768]{1,0:T(8,128)S(1)} fusion(bf16[1536,2048]{1,0:T(8,128)(2,1)} %bitcast.40, bf16[1,2048,768]{2,1,0:T(8,128)(2,1)} %param.13), kind=kOutput, calls=%fused_computation.11 | convolution fusion | flops 4831838208 | bytes 14155776 | tf_op jit(solution)/shard_map/dot_general | solution.py:36
  356.0 5.6 multiply_convert_fusion.1
  361.6 5.3 convolution_convert_fusion.1
  367.0 4.8 multiply_convert_fusion
  371.7 0.0 reduce-scatter.2.cloned.1.call-update
  371.7 224.4 %reduce-scatter.2.cloned.1.call-done = bf16[128,2048]{1,0:T(8,128)(2,1)} async-done(((bf16[2048,2048]{1,0:T(8,128)(2,1)}), bf16[128,2048]{1,0:T(8,128)(2,1)}) %reduce-scatter.2.cloned.1.call-update) | async-done | bytes 524304 | tf_op jit(solution)/shard_map/reduce_scatter | solution.py:79
  (31 shorter events, 0.1 us)
Async XLA Ops:
  6.5 355.1 %copy-start = (bf16[1,768,2048]{2,1,0:T(8,128)(2,1)S(1)}, bf16[1,768,2048]{2,1,0:T(8,128)(2,1)}, u32[]{:S(2)}) copy-start(bf16[1,768,2048]{2,1,0:T(8,128)(2,1)} %param.15) | copy-start | bytes 9437188
  6.5 589.6 %reduce-scatter.2.cloned.1.call-start = ((), (), s32[]{:S(2)}) async-start(), calls=%async_computation.1 | async-start | bytes 8912896 | tf_op jit(solution)/shard_map/reduce_scatter | solution.py:79
  56.1 2.0 copy-start.3
  58.1 2.6 copy-start.1
  60.8 13.1 %collective-permute-start = (bf16[128,2048]{1,0:T(8,128)(2,1)}, bf16[128,2048]{1,0:T(8,128)(2,1)}, u32[]{:S(2)}, u32[]{:S(2)}) collective-permute-start(bf16[128,2048]{1,0:T(8,128)(2,1)} %get-tuple-element.195), channel_id=1, source_target_pairs={{15,0},{0,1},{1,2},{2,3},{3,4},{4,5},{5,6},{6,7},{7,8},{8,9},{9,10... | collective-permute-start | bytes 1572872 | tf_op jit(solution)/shard_map/while/body/eval_jaxpr/ppermute | solution.py:12
  77.8 13.1 %collective-permute-start = (bf16[128,2048]{1,0:T(8,128)(2,1)}, bf16[128,2048]{1,0:T(8,128)(2,1)}, u32[]{:S(2)}, u32[]{:S(2)}) collective-permute-start(bf16[128,2048]{1,0:T(8,128)(2,1)} %get-tuple-element.195), channel_id=1, source_target_pairs={{15,0},{0,1},{1,2},{2,3},{3,4},{4,5},{5,6},{6,7},{7,8},{8,9},{9,10... | collective-permute-start | bytes 1572872 | tf_op jit(solution)/shard_map/while/body/eval_jaxpr/ppermute | solution.py:12
  94.9 13.5 %collective-permute-start = (bf16[128,2048]{1,0:T(8,128)(2,1)}, bf16[128,2048]{1,0:T(8,128)(2,1)}, u32[]{:S(2)}, u32[]{:S(2)}) collective-permute-start(bf16[128,2048]{1,0:T(8,128)(2,1)} %get-tuple-element.195), channel_id=1, source_target_pairs={{15,0},{0,1},{1,2},{2,3},{3,4},{4,5},{5,6},{6,7},{7,8},{8,9},{9,10... | collective-permute-start | bytes 1572872 | tf_op jit(solution)/shard_map/while/body/eval_jaxpr/ppermute | solution.py:12
  112.4 14.7 %collective-permute-start = (bf16[128,2048]{1,0:T(8,128)(2,1)}, bf16[128,2048]{1,0:T(8,128)(2,1)}, u32[]{:S(2)}, u32[]{:S(2)}) collective-permute-start(bf16[128,2048]{1,0:T(8,128)(2,1)} %get-tuple-element.195), channel_id=1, source_target_pairs={{15,0},{0,1},{1,2},{2,3},{3,4},{4,5},{5,6},{6,7},{7,8},{8,9},{9,10... | collective-permute-start | bytes 1572872 | tf_op jit(solution)/shard_map/while/body/eval_jaxpr/ppermute | solution.py:12
  131.0 15.8 %collective-permute-start = (bf16[128,2048]{1,0:T(8,128)(2,1)}, bf16[128,2048]{1,0:T(8,128)(2,1)}, u32[]{:S(2)}, u32[]{:S(2)}) collective-permute-start(bf16[128,2048]{1,0:T(8,128)(2,1)} %get-tuple-element.195), channel_id=1, source_target_pairs={{15,0},{0,1},{1,2},{2,3},{3,4},{4,5},{5,6},{6,7},{7,8},{8,9},{9,10... | collective-permute-start | bytes 1572872 | tf_op jit(solution)/shard_map/while/body/eval_jaxpr/ppermute | solution.py:12
  150.7 17.0 %collective-permute-start = (bf16[128,2048]{1,0:T(8,128)(2,1)}, bf16[128,2048]{1,0:T(8,128)(2,1)}, u32[]{:S(2)}, u32[]{:S(2)}) collective-permute-start(bf16[128,2048]{1,0:T(8,128)(2,1)} %get-tuple-element.195), channel_id=1, source_target_pairs={{15,0},{0,1},{1,2},{2,3},{3,4},{4,5},{5,6},{6,7},{7,8},{8,9},{9,10... | collective-permute-start | bytes 1572872 | tf_op jit(solution)/shard_map/while/body/eval_jaxpr/ppermute | solution.py:12
  171.6 18.1 %collective-permute-start = (bf16[128,2048]{1,0:T(8,128)(2,1)}, bf16[128,2048]{1,0:T(8,128)(2,1)}, u32[]{:S(2)}, u32[]{:S(2)}) collective-permute-start(bf16[128,2048]{1,0:T(8,128)(2,1)} %get-tuple-element.195), channel_id=1, source_target_pairs={{15,0},{0,1},{1,2},{2,3},{3,4},{4,5},{5,6},{6,7},{7,8},{8,9},{9,10... | collective-permute-start | bytes 1572872 | tf_op jit(solution)/shard_map/while/body/eval_jaxpr/ppermute | solution.py:12
  193.6 18.2 %collective-permute-start = (bf16[128,2048]{1,0:T(8,128)(2,1)}, bf16[128,2048]{1,0:T(8,128)(2,1)}, u32[]{:S(2)}, u32[]{:S(2)}) collective-permute-start(bf16[128,2048]{1,0:T(8,128)(2,1)} %get-tuple-element.195), channel_id=1, source_target_pairs={{15,0},{0,1},{1,2},{2,3},{3,4},{4,5},{5,6},{6,7},{7,8},{8,9},{9,10... | collective-permute-start | bytes 1572872 | tf_op jit(solution)/shard_map/while/body/eval_jaxpr/ppermute | solution.py:12
  215.7 17.4 %collective-permute-start = (bf16[128,2048]{1,0:T(8,128)(2,1)}, bf16[128,2048]{1,0:T(8,128)(2,1)}, u32[]{:S(2)}, u32[]{:S(2)}) collective-permute-start(bf16[128,2048]{1,0:T(8,128)(2,1)} %get-tuple-element.195), channel_id=1, source_target_pairs={{15,0},{0,1},{1,2},{2,3},{3,4},{4,5},{5,6},{6,7},{7,8},{8,9},{9,10... | collective-permute-start | bytes 1572872 | tf_op jit(solution)/shard_map/while/body/eval_jaxpr/ppermute | solution.py:12
  237.0 16.5 %collective-permute-start = (bf16[128,2048]{1,0:T(8,128)(2,1)}, bf16[128,2048]{1,0:T(8,128)(2,1)}, u32[]{:S(2)}, u32[]{:S(2)}) collective-permute-start(bf16[128,2048]{1,0:T(8,128)(2,1)} %get-tuple-element.195), channel_id=1, source_target_pairs={{15,0},{0,1},{1,2},{2,3},{3,4},{4,5},{5,6},{6,7},{7,8},{8,9},{9,10... | collective-permute-start | bytes 1572872 | tf_op jit(solution)/shard_map/while/body/eval_jaxpr/ppermute | solution.py:12
  257.4 15.7 %collective-permute-start = (bf16[128,2048]{1,0:T(8,128)(2,1)}, bf16[128,2048]{1,0:T(8,128)(2,1)}, u32[]{:S(2)}, u32[]{:S(2)}) collective-permute-start(bf16[128,2048]{1,0:T(8,128)(2,1)} %get-tuple-element.195), channel_id=1, source_target_pairs={{15,0},{0,1},{1,2},{2,3},{3,4},{4,5},{5,6},{6,7},{7,8},{8,9},{9,10... | collective-permute-start | bytes 1572872 | tf_op jit(solution)/shard_map/while/body/eval_jaxpr/ppermute | solution.py:12
  277.1 14.8 %collective-permute-start = (bf16[128,2048]{1,0:T(8,128)(2,1)}, bf16[128,2048]{1,0:T(8,128)(2,1)}, u32[]{:S(2)}, u32[]{:S(2)}) collective-permute-start(bf16[128,2048]{1,0:T(8,128)(2,1)} %get-tuple-element.195), channel_id=1, source_target_pairs={{15,0},{0,1},{1,2},{2,3},{3,4},{4,5},{5,6},{6,7},{7,8},{8,9},{9,10... | collective-permute-start | bytes 1572872 | tf_op jit(solution)/shard_map/while/body/eval_jaxpr/ppermute | solution.py:12
  295.8 13.9 %collective-permute-start = (bf16[128,2048]{1,0:T(8,128)(2,1)}, bf16[128,2048]{1,0:T(8,128)(2,1)}, u32[]{:S(2)}, u32[]{:S(2)}) collective-permute-start(bf16[128,2048]{1,0:T(8,128)(2,1)} %get-tuple-element.195), channel_id=1, source_target_pairs={{15,0},{0,1},{1,2},{2,3},{3,4},{4,5},{5,6},{6,7},{7,8},{8,9},{9,10... | collective-permute-start | bytes 1572872 | tf_op jit(solution)/shard_map/while/body/eval_jaxpr/ppermute | solution.py:12
  313.7 13.1 %collective-permute-start = (bf16[128,2048]{1,0:T(8,128)(2,1)}, bf16[128,2048]{1,0:T(8,128)(2,1)}, u32[]{:S(2)}, u32[]{:S(2)}) collective-permute-start(bf16[128,2048]{1,0:T(8,128)(2,1)} %get-tuple-element.195), channel_id=1, source_target_pairs={{15,0},{0,1},{1,2},{2,3},{3,4},{4,5},{5,6},{6,7},{7,8},{8,9},{9,10... | collective-permute-start | bytes 1572872 | tf_op jit(solution)/shard_map/while/body/eval_jaxpr/ppermute | solution.py:12
  330.7 13.1 %collective-permute-start = (bf16[128,2048]{1,0:T(8,128)(2,1)}, bf16[128,2048]{1,0:T(8,128)(2,1)}, u32[]{:S(2)}, u32[]{:S(2)}) collective-permute-start(bf16[128,2048]{1,0:T(8,128)(2,1)} %get-tuple-element.195), channel_id=1, source_target_pairs={{15,0},{0,1},{1,2},{2,3},{3,4},{4,5},{5,6},{6,7},{7,8},{8,9},{9,10... | collective-permute-start | bytes 1572872 | tf_op jit(solution)/shard_map/while/body/eval_jaxpr/ppermute | solution.py:12
  347.8 8.2 %copy-start.2 = (bf16[16,96,2048]{2,1,0:T(8,128)(2,1)S(1)}, bf16[16,96,2048]{2,1,0:T(8,128)(2,1)}, u32[]{:S(2)}) copy-start(bf16[16,96,2048]{2,1,0:T(8,128)(2,1)} %get-tuple-element.138) | copy-start | bytes 18874372
  347.8 8.2 %copy-start.6 = (bf16[1,2048,768]{2,1,0:T(8,128)(2,1)S(1)}, bf16[1,2048,768]{2,1,0:T(8,128)(2,1)}, u32[]{:S(2)}) copy-start(bf16[1,2048,768]{2,1,0:T(8,128)(2,1)} %param.14) | copy-start | bytes 9437188
  361.6 5.3 copy-start.4
  361.6 5.3 copy-start.5
Sparse Core Ops, SparseCore 0:
  371.9 224.2 reduce-scatter.1
where the time goes:
time: 605 us; the launch traced here: 603 us
  waiting for transfers between devices  452 us (75%)
  matrix products  55 us (9%)
  blocking collectives  44.7 us (7%)
  local copies, waits for them, and re-layouts  31.7 us (5%)
  between operations  13.5 us (2%)
    ppermute x15, waiting for transfers between devices, passed_along(): return lax.ppermute(block, axis, route)  228 us
    reduce_scatter x1, waiting for transfers between devices, local(): lax.psum_scatter((back * column[:, :, None]).reshape(spanned * local_rows...  224 us
    all_gather x1, blocking collectives, local(): gathered = lax.all_gather(dense, 'expert', axis=0, tiled=True)  44.7 us
    dot_general x16, matrix products, place_block(): jnp.dot(picked, carried, preferred_element_type=jnp.float32)  31.1 us
    while x15, local copies, waits for them, and re-layouts  28.2 us
  transfers between devices with their start and end apart: 16, of which 16 were waited for; matrix products, arithmetic and copies ran while one was open for 0% of the time, Pallas kernels for 0%

commit v1 on v0

--- a/solution.py
+++ b/solution.py
@@ -4,6 +4,13 @@
 from jax.sharding import PartitionSpec as P
 
 eps_value = 1e-06
+
+
+def shape_the_rates(page, across):
+    taken_in = lax.axis_size(across)
+    carry = jnp.stack([page] * taken_in, 0)
+    n_now = lax.all_to_all(carry, across, 0, 0)
+    return jnp.concatenate(n_now, 0)
 
 
 def passed_along(block, axis, distance):
@@ -57,7 +64,7 @@
     down_matrix = w_down[0]
     normed = normalize(tokens, gain)
     dense = gate_dense(expert_ids, gate_values, group)
-    gathered = lax.all_gather(dense, "expert", axis=0, tiled=True)
+    gathered = shape_the_rates(dense, "expert")
     column = lax.dynamic_slice_in_dim(gathered, position, 1, 1).reshape(group, local_rows)
     table = dispatch_table(column, capacity)
     buffer = jnp.zeros((group, capacity, width), jnp.bfloat16)

time: 605 us -> 573 us (0.947)
  blocking collectives: 44.7 us -> 0 us
  starting transfers between devices: 0.04 us -> 12 us
    all_gather x1 -> x0, blocking collectives: 44.7 us -> none  [local(): gathered = lax.all_gather(dense, 'expert', axis=0, tiled=True)]
    all_to_all x0 -> x1, starting transfers between devices: none -> 11.2 us  [shape_the_rates(): n_now = lax.all_to_all(carry, across, 0, 0)]
    all_to_all x0 -> x1, waiting for transfers between devices: none -> 7.23 us  [shape_the_rates(): n_now = lax.all_to_all(carry, across, 0, 0)]
    ppermute x15, waiting for transfers between devices: 228 us -> 221 us  [passed_along(): return lax.ppermute(block, axis, route)]
  transfers between devices with their start and end apart: 16 -> 17, of which waited for: 16 -> 17; matrix products, arithmetic and copies ran while one was open for 0% -> 1% of each run, Pallas kernels for 0% -> 0%
where the time goes in v1:
time: 573 us; the launch traced here: 571 us
  waiting for transfers between devices  452 us (79%)
  matrix products  55 us (10%)
  local copies, waits for them, and re-layouts  32.3 us (6%)
  between operations  13.5 us (2%)
  starting transfers between devices  12 us (2%)
  other arithmetic  6.54 us (1%)
    reduce_scatter x1, waiting for transfers between devices, local(): lax.psum_scatter((back * column[:, :, None]).reshape(spanned * local_rows...  223 us
    ppermute x15, waiting for transfers between devices, passed_along(): return lax.ppermute(block, axis, route)  221 us
    dot_general x16, matrix products, place_block(): jnp.dot(picked, carried, preferred_element_type=jnp.float32)  31.1 us
    while x15, local copies, waits for them, and re-layouts  28.2 us
  transfers between devices with their start and end apart: 17, of which 17 were waited for; matrix products, arithmetic and copies ran while one was open for 1% of the time, Pallas kernels for 0%

profile of v1, /device:TPU:2, one launch (start us, length us, event | category | flops | bytes accessed | tf_op | source)
XLA Modules:
  0.0 571.0 jit_solution(11115032741991832399)
XLA Ops:
  6.5 0.9 select_reduce_fusion
  7.4 0.7 stack.2
  8.1 11.2 %all-to-all-start = ((f32[16,128,16]{1,2,0:T(8,128)}), f32[16,128,16]{1,2,0:T(8,128)S(1)}, u32[]{:S(2)}, u32[]{:S(2)}) async-start(f32[16,128,16]{1,2,0:T(8,128)} %stack.2), calls=%async_computation | async-start | bytes 262144 | tf_op jit(solution)/shard_map/all_to_all | solution.py:12
  19.3 1.2 fusion.11
  20.6 2.0 fusion.13
  22.6 0.6 iota_convert_fusion
  23.2 7.2 %all-to-all-done = f32[16,128,16]{1,2,0:T(8,128)S(1)} async-done(((f32[16,128,16]{1,2,0:T(8,128)}), f32[16,128,16]{1,2,0:T(8,128)S(1)}, u32[]{:S(2)}, u32[]{:S(2)}) %all-to-all-start) | async-done | bytes 131104 | tf_op jit(solution)/shard_map/all_to_all | solution.py:12
  30.4 0.6 broadcast_compare_fusion
  31.0 0.3 reduce_window_sum.11
  31.3 1.0 fusion.17
  32.3 0.8 broadcast_in_dim.24
  33.4 2.6 copy-done.1
  36.0 281.0 %while.17 = (s32[]{:T(128)}, bf16[16,96,2048]{2,1,0:T(8,128)(2,1)}, bf16[128,2048]{1,0:T(8,128)(2,1)}, s32[]{:T(128)}, bf16[16,96,128]{2,1,0:T(8,128)(2,1)S(1)},...) while((s32[]{:T(128)}, bf16[16,96,2048]{2,1,0:T(8,128)(2,1)}, bf16[128,2048]{1,0:T(8,128)(2,1)}, s32[]{:T(128)}, ...), condition=%wide.region_4.5_spmd, body=%wide.region_3.4_spmd.sunk | while | flops 50528272 | bytes 4089120 | solution.py:79
  36.0 0.8 collective-permute-start
  36.7 15.4 %collective-permute-done = bf16[128,2048]{1,0:T(8,128)(2,1)} collective-permute-done((bf16[128,2048]{1,0:T(8,128)(2,1)}, bf16[128,2048]{1,0:T(8,128)(2,1)}, u32[]{:S(2)}, u32[]{:S(2)}) %collective-permute-start) | collective-permute-done | bytes 524320 | tf_op jit(solution)/shard_map/while/body/eval_jaxpr/ppermute | solution.py:19
  52.2 1.9 copy.28
  54.0 2.0 fusion.30
  56.1 15.3 %collective-permute-done = bf16[128,2048]{1,0:T(8,128)(2,1)} collective-permute-done((bf16[128,2048]{1,0:T(8,128)(2,1)}, bf16[128,2048]{1,0:T(8,128)(2,1)}, u32[]{:S(2)}, u32[]{:S(2)}) %collective-permute-start) | collective-permute-done | bytes 524320 | tf_op jit(solution)/shard_map/while/body/eval_jaxpr/ppermute | solution.py:19
  71.4 1.9 copy.28
  73.3 2.1 fusion.30
  75.4 14.4 %collective-permute-done = bf16[128,2048]{1,0:T(8,128)(2,1)} collective-permute-done((bf16[128,2048]{1,0:T(8,128)(2,1)}, bf16[128,2048]{1,0:T(8,128)(2,1)}, u32[]{:S(2)}, u32[]{:S(2)}) %collective-permute-start) | collective-permute-done | bytes 524320 | tf_op jit(solution)/shard_map/while/body/eval_jaxpr/ppermute | solution.py:19
  89.8 1.9 copy.28
  91.7 2.1 fusion.30
  93.7 13.6 %collective-permute-done = bf16[128,2048]{1,0:T(8,128)(2,1)} collective-permute-done((bf16[128,2048]{1,0:T(8,128)(2,1)}, bf16[128,2048]{1,0:T(8,128)(2,1)}, u32[]{:S(2)}, u32[]{:S(2)}) %collective-permute-start) | collective-permute-done | bytes 524320 | tf_op jit(solution)/shard_map/while/body/eval_jaxpr/ppermute | solution.py:19
  107.3 1.9 copy.28
  109.2 2.1 fusion.30
  111.3 13.1 %collective-permute-done = bf16[128,2048]{1,0:T(8,128)(2,1)} collective-permute-done((bf16[128,2048]{1,0:T(8,128)(2,1)}, bf16[128,2048]{1,0:T(8,128)(2,1)}, u32[]{:S(2)}, u32[]{:S(2)}) %collective-permute-start) | collective-permute-done | bytes 524320 | tf_op jit(solution)/shard_map/while/body/eval_jaxpr/ppermute | solution.py:19
  124.4 1.9 copy.28
  126.3 2.1 fusion.30
  128.3 13.1 %collective-permute-done = bf16[128,2048]{1,0:T(8,128)(2,1)} collective-permute-done((bf16[128,2048]{1,0:T(8,128)(2,1)}, bf16[128,2048]{1,0:T(8,128)(2,1)}, u32[]{:S(2)}, u32[]{:S(2)}) %collective-permute-start) | collective-permute-done | bytes 524320 | tf_op jit(solution)/shard_map/while/body/eval_jaxpr/ppermute | solution.py:19
  141.5 1.9 copy.28
  143.3 2.0 fusion.30
  145.4 13.1 %collective-permute-done = bf16[128,2048]{1,0:T(8,128)(2,1)} collective-permute-done((bf16[128,2048]{1,0:T(8,128)(2,1)}, bf16[128,2048]{1,0:T(8,128)(2,1)}, u32[]{:S(2)}, u32[]{:S(2)}) %collective-permute-start) | collective-permute-done | bytes 524320 | tf_op jit(solution)/shard_map/while/body/eval_jaxpr/ppermute | solution.py:19
  158.5 1.9 copy.28
  160.4 2.0 fusion.30
  162.4 13.1 %collective-permute-done = bf16[128,2048]{1,0:T(8,128)(2,1)} collective-permute-done((bf16[128,2048]{1,0:T(8,128)(2,1)}, bf16[128,2048]{1,0:T(8,128)(2,1)}, u32[]{:S(2)}, u32[]{:S(2)}) %collective-permute-start) | collective-permute-done | bytes 524320 | tf_op jit(solution)/shard_map/while/body/eval_jaxpr/ppermute | solution.py:19
  175.5 1.9 copy.28
  177.4 2.0 fusion.30
  179.4 13.4 %collective-permute-done = bf16[128,2048]{1,0:T(8,128)(2,1)} collective-permute-done((bf16[128,2048]{1,0:T(8,128)(2,1)}, bf16[128,2048]{1,0:T(8,128)(2,1)}, u32[]{:S(2)}, u32[]{:S(2)}) %collective-permute-start) | collective-permute-done | bytes 524320 | tf_op jit(solution)/shard_map/while/body/eval_jaxpr/ppermute | solution.py:19
  192.9 1.9 copy.28
  194.7 2.1 fusion.30
  196.8 14.6 %collective-permute-done = bf16[128,2048]{1,0:T(8,128)(2,1)} collective-permute-done((bf16[128,2048]{1,0:T(8,128)(2,1)}, bf16[128,2048]{1,0:T(8,128)(2,1)}, u32[]{:S(2)}, u32[]{:S(2)}) %collective-permute-start) | collective-permute-done | bytes 524320 | tf_op jit(solution)/shard_map/while/body/eval_jaxpr/ppermute | solution.py:19
  211.4 1.9 copy.28
  213.2 2.1 fusion.30
  215.3 15.7 %collective-permute-done = bf16[128,2048]{1,0:T(8,128)(2,1)} collective-permute-done((bf16[128,2048]{1,0:T(8,128)(2,1)}, bf16[128,2048]{1,0:T(8,128)(2,1)}, u32[]{:S(2)}, u32[]{:S(2)}) %collective-permute-start) | collective-permute-done | bytes 524320 | tf_op jit(solution)/shard_map/while/body/eval_jaxpr/ppermute | solution.py:19
  231.0 1.9 copy.28
  232.9 2.1 fusion.30
  235.0 16.9 %collective-permute-done = bf16[128,2048]{1,0:T(8,128)(2,1)} collective-permute-done((bf16[128,2048]{1,0:T(8,128)(2,1)}, bf16[128,2048]{1,0:T(8,128)(2,1)}, u32[]{:S(2)}, u32[]{:S(2)}) %collective-permute-start) | collective-permute-done | bytes 524320 | tf_op jit(solution)/shard_map/while/body/eval_jaxpr/ppermute | solution.py:19
  251.8 1.9 copy.28
  253.7 2.0 fusion.30
  255.8 18.0 %collective-permute-done = bf16[128,2048]{1,0:T(8,128)(2,1)} collective-permute-done((bf16[128,2048]{1,0:T(8,128)(2,1)}, bf16[128,2048]{1,0:T(8,128)(2,1)}, u32[]{:S(2)}, u32[]{:S(2)}) %collective-permute-start) | collective-permute-done | bytes 524320 | tf_op jit(solution)/shard_map/while/body/eval_jaxpr/ppermute | solution.py:19
  273.8 1.9 copy.28
  275.6 2.1 fusion.30
  277.7 18.3 %collective-permute-done = bf16[128,2048]{1,0:T(8,128)(2,1)} collective-permute-done((bf16[128,2048]{1,0:T(8,128)(2,1)}, bf16[128,2048]{1,0:T(8,128)(2,1)}, u32[]{:S(2)}, u32[]{:S(2)}) %collective-permute-start) | collective-permute-done | bytes 524320 | tf_op jit(solution)/shard_map/while/body/eval_jaxpr/ppermute | solution.py:19
  296.0 1.9 copy.28
  297.9 2.1 fusion.30
  300.0 13.1 %collective-permute-done = bf16[128,2048]{1,0:T(8,128)(2,1)} collective-permute-done((bf16[128,2048]{1,0:T(8,128)(2,1)}, bf16[128,2048]{1,0:T(8,128)(2,1)}, u32[]{:S(2)}, u32[]{:S(2)}) %collective-permute-start) | collective-permute-done | bytes 524320 | tf_op jit(solution)/shard_map/while/body/eval_jaxpr/ppermute | solution.py:19
  313.1 1.9 copy.28
  314.9 2.1 fusion.30
  317.0 8.2 %fusion.7 = f32[1536,768]{1,0:T(8,128)S(1)} fusion(bf16[1536,2048]{1,0:T(8,128)(2,1)} %bitcast.45, bf16[1,2048,768]{2,1,0:T(8,128)(2,1)} %param.13), kind=kOutput, calls=%fused_computation.11 | convolution fusion | flops 4831838208 | bytes 14155776 | tf_op jit(solution)/shard_map/dot_general | solution.py:43
  325.2 5.6 multiply_convert_fusion.1
  330.9 5.3 convolution_convert_fusion.1
  336.2 4.8 multiply_convert_fusion
  341.0 223.2 %reduce-scatter.2.cloned.1.call-done = bf16[128,2048]{1,0:T(8,128)(2,1)} async-done(((bf16[2048,2048]{1,0:T(8,128)(2,1)}), bf16[128,2048]{1,0:T(8,128)(2,1)}) %reduce-scatter.2.cloned.1.call-update) | async-done | bytes 524304 | tf_op jit(solution)/shard_map/reduce_scatter | solution.py:86
  (34 shorter events, 0.4 us)
Async XLA Ops:
  6.5 324.3 %copy-start = (bf16[1,768,2048]{2,1,0:T(8,128)(2,1)S(1)}, bf16[1,768,2048]{2,1,0:T(8,128)(2,1)}, u32[]{:S(2)}) copy-start(bf16[1,768,2048]{2,1,0:T(8,128)(2,1)} %param.15) | copy-start | bytes 9437188
  8.1 22.3 %all-to-all-start = ((f32[16,128,16]{1,2,0:T(8,128)}), f32[16,128,16]{1,2,0:T(8,128)S(1)}, u32[]{:S(2)}, u32[]{:S(2)}) async-start(f32[16,128,16]{1,2,0:T(8,128)} %stack.2), calls=%async_computation | async-start | bytes 262144 | tf_op jit(solution)/shard_map/all_to_all | solution.py:12
  19.3 544.9 %reduce-scatter.2.cloned.1.call-start = ((), (), s32[]{:S(2)}) async-start(), calls=%async_computation.2 | async-start | bytes 8912896 | tf_op jit(solution)/shard_map/reduce_scatter | solution.py:86
  31.3 1.8 copy-start.3
  33.3 2.7 copy-start.1
  36.0 16.2 %collective-permute-start = (bf16[128,2048]{1,0:T(8,128)(2,1)}, bf16[128,2048]{1,0:T(8,128)(2,1)}, u32[]{:S(2)}, u32[]{:S(2)}) collective-permute-start(bf16[128,2048]{1,0:T(8,128)(2,1)} %get-tuple-element.195), channel_id=1, source_target_pairs={{15,0},{0,1},{1,2},{2,3},{3,4},{4,5},{5,6},{6,7},{7,8},{8,9},{9,10... | collective-permute-start | bytes 1572872 | tf_op jit(solution)/shard_map/while/body/eval_jaxpr/ppermute | solution.py:19
  56.1 15.3 %collective-permute-start = (bf16[128,2048]{1,0:T(8,128)(2,1)}, bf16[128,2048]{1,0:T(8,128)(2,1)}, u32[]{:S(2)}, u32[]{:S(2)}) collective-permute-start(bf16[128,2048]{1,0:T(8,128)(2,1)} %get-tuple-element.195), channel_id=1, source_target_pairs={{15,0},{0,1},{1,2},{2,3},{3,4},{4,5},{5,6},{6,7},{7,8},{8,9},{9,10... | collective-permute-start | bytes 1572872 | tf_op jit(solution)/shard_map/while/body/eval_jaxpr/ppermute | solution.py:19
  75.4 14.4 %collective-permute-start = (bf16[128,2048]{1,0:T(8,128)(2,1)}, bf16[128,2048]{1,0:T(8,128)(2,1)}, u32[]{:S(2)}, u32[]{:S(2)}) collective-permute-start(bf16[128,2048]{1,0:T(8,128)(2,1)} %get-tuple-element.195), channel_id=1, source_target_pairs={{15,0},{0,1},{1,2},{2,3},{3,4},{4,5},{5,6},{6,7},{7,8},{8,9},{9,10... | collective-permute-start | bytes 1572872 | tf_op jit(solution)/shard_map/while/body/eval_jaxpr/ppermute | solution.py:19
  93.7 13.6 %collective-permute-start = (bf16[128,2048]{1,0:T(8,128)(2,1)}, bf16[128,2048]{1,0:T(8,128)(2,1)}, u32[]{:S(2)}, u32[]{:S(2)}) collective-permute-start(bf16[128,2048]{1,0:T(8,128)(2,1)} %get-tuple-element.195), channel_id=1, source_target_pairs={{15,0},{0,1},{1,2},{2,3},{3,4},{4,5},{5,6},{6,7},{7,8},{8,9},{9,10... | collective-permute-start | bytes 1572872 | tf_op jit(solution)/shard_map/while/body/eval_jaxpr/ppermute | solution.py:19
  111.3 13.1 %collective-permute-start = (bf16[128,2048]{1,0:T(8,128)(2,1)}, bf16[128,2048]{1,0:T(8,128)(2,1)}, u32[]{:S(2)}, u32[]{:S(2)}) collective-permute-start(bf16[128,2048]{1,0:T(8,128)(2,1)} %get-tuple-element.195), channel_id=1, source_target_pairs={{15,0},{0,1},{1,2},{2,3},{3,4},{4,5},{5,6},{6,7},{7,8},{8,9},{9,10... | collective-permute-start | bytes 1572872 | tf_op jit(solution)/shard_map/while/body/eval_jaxpr/ppermute | solution.py:19
  128.3 13.1 %collective-permute-start = (bf16[128,2048]{1,0:T(8,128)(2,1)}, bf16[128,2048]{1,0:T(8,128)(2,1)}, u32[]{:S(2)}, u32[]{:S(2)}) collective-permute-start(bf16[128,2048]{1,0:T(8,128)(2,1)} %get-tuple-element.195), channel_id=1, source_target_pairs={{15,0},{0,1},{1,2},{2,3},{3,4},{4,5},{5,6},{6,7},{7,8},{8,9},{9,10... | collective-permute-start | bytes 1572872 | tf_op jit(solution)/shard_map/while/body/eval_jaxpr/ppermute | solution.py:19
  145.4 13.1 %collective-permute-start = (bf16[128,2048]{1,0:T(8,128)(2,1)}, bf16[128,2048]{1,0:T(8,128)(2,1)}, u32[]{:S(2)}, u32[]{:S(2)}) collective-permute-start(bf16[128,2048]{1,0:T(8,128)(2,1)} %get-tuple-element.195), channel_id=1, source_target_pairs={{15,0},{0,1},{1,2},{2,3},{3,4},{4,5},{5,6},{6,7},{7,8},{8,9},{9,10... | collective-permute-start | bytes 1572872 | tf_op jit(solution)/shard_map/while/body/eval_jaxpr/ppermute | solution.py:19
  162.4 13.1 %collective-permute-start = (bf16[128,2048]{1,0:T(8,128)(2,1)}, bf16[128,2048]{1,0:T(8,128)(2,1)}, u32[]{:S(2)}, u32[]{:S(2)}) collective-permute-start(bf16[128,2048]{1,0:T(8,128)(2,1)} %get-tuple-element.195), channel_id=1, source_target_pairs={{15,0},{0,1},{1,2},{2,3},{3,4},{4,5},{5,6},{6,7},{7,8},{8,9},{9,10... | collective-permute-start | bytes 1572872 | tf_op jit(solution)/shard_map/while/body/eval_jaxpr/ppermute | solution.py:19
  179.4 13.4 %collective-permute-start = (bf16[128,2048]{1,0:T(8,128)(2,1)}, bf16[128,2048]{1,0:T(8,128)(2,1)}, u32[]{:S(2)}, u32[]{:S(2)}) collective-permute-start(bf16[128,2048]{1,0:T(8,128)(2,1)} %get-tuple-element.195), channel_id=1, source_target_pairs={{15,0},{0,1},{1,2},{2,3},{3,4},{4,5},{5,6},{6,7},{7,8},{8,9},{9,10... | collective-permute-start | bytes 1572872 | tf_op jit(solution)/shard_map/while/body/eval_jaxpr/ppermute | solution.py:19
  196.8 14.6 %collective-permute-start = (bf16[128,2048]{1,0:T(8,128)(2,1)}, bf16[128,2048]{1,0:T(8,128)(2,1)}, u32[]{:S(2)}, u32[]{:S(2)}) collective-permute-start(bf16[128,2048]{1,0:T(8,128)(2,1)} %get-tuple-element.195), channel_id=1, source_target_pairs={{15,0},{0,1},{1,2},{2,3},{3,4},{4,5},{5,6},{6,7},{7,8},{8,9},{9,10... | collective-permute-start | bytes 1572872 | tf_op jit(solution)/shard_map/while/body/eval_jaxpr/ppermute | solution.py:19
  215.3 15.7 %collective-permute-start = (bf16[128,2048]{1,0:T(8,128)(2,1)}, bf16[128,2048]{1,0:T(8,128)(2,1)}, u32[]{:S(2)}, u32[]{:S(2)}) collective-permute-start(bf16[128,2048]{1,0:T(8,128)(2,1)} %get-tuple-element.195), channel_id=1, source_target_pairs={{15,0},{0,1},{1,2},{2,3},{3,4},{4,5},{5,6},{6,7},{7,8},{8,9},{9,10... | collective-permute-start | bytes 1572872 | tf_op jit(solution)/shard_map/while/body/eval_jaxpr/ppermute | solution.py:19
  235.0 16.9 %collective-permute-start = (bf16[128,2048]{1,0:T(8,128)(2,1)}, bf16[128,2048]{1,0:T(8,128)(2,1)}, u32[]{:S(2)}, u32[]{:S(2)}) collective-permute-start(bf16[128,2048]{1,0:T(8,128)(2,1)} %get-tuple-element.195), channel_id=1, source_target_pairs={{15,0},{0,1},{1,2},{2,3},{3,4},{4,5},{5,6},{6,7},{7,8},{8,9},{9,10... | collective-permute-start | bytes 1572872 | tf_op jit(solution)/shard_map/while/body/eval_jaxpr/ppermute | solution.py:19
  255.8 18.0 %collective-permute-start = (bf16[128,2048]{1,0:T(8,128)(2,1)}, bf16[128,2048]{1,0:T(8,128)(2,1)}, u32[]{:S(2)}, u32[]{:S(2)}) collective-permute-start(bf16[128,2048]{1,0:T(8,128)(2,1)} %get-tuple-element.195), channel_id=1, source_target_pairs={{15,0},{0,1},{1,2},{2,3},{3,4},{4,5},{5,6},{6,7},{7,8},{8,9},{9,10... | collective-permute-start | bytes 1572872 | tf_op jit(solution)/shard_map/while/body/eval_jaxpr/ppermute | solution.py:19
  277.7 18.3 %collective-permute-start = (bf16[128,2048]{1,0:T(8,128)(2,1)}, bf16[128,2048]{1,0:T(8,128)(2,1)}, u32[]{:S(2)}, u32[]{:S(2)}) collective-permute-start(bf16[128,2048]{1,0:T(8,128)(2,1)} %get-tuple-element.195), channel_id=1, source_target_pairs={{15,0},{0,1},{1,2},{2,3},{3,4},{4,5},{5,6},{6,7},{7,8},{8,9},{9,10... | collective-permute-start | bytes 1572872 | tf_op jit(solution)/shard_map/while/body/eval_jaxpr/ppermute | solution.py:19
  300.0 13.1 %collective-permute-start = (bf16[128,2048]{1,0:T(8,128)(2,1)}, bf16[128,2048]{1,0:T(8,128)(2,1)}, u32[]{:S(2)}, u32[]{:S(2)}) collective-permute-start(bf16[128,2048]{1,0:T(8,128)(2,1)} %get-tuple-element.195), channel_id=1, source_target_pairs={{15,0},{0,1},{1,2},{2,3},{3,4},{4,5},{5,6},{6,7},{7,8},{8,9},{9,10... | collective-permute-start | bytes 1572872 | tf_op jit(solution)/shard_map/while/body/eval_jaxpr/ppermute | solution.py:19
  317.0 8.2 %copy-start.2 = (bf16[16,96,2048]{2,1,0:T(8,128)(2,1)S(1)}, bf16[16,96,2048]{2,1,0:T(8,128)(2,1)}, u32[]{:S(2)}) copy-start(bf16[16,96,2048]{2,1,0:T(8,128)(2,1)} %get-tuple-element.138) | copy-start | bytes 18874372
  317.0 8.2 %copy-start.6 = (bf16[1,2048,768]{2,1,0:T(8,128)(2,1)S(1)}, bf16[1,2048,768]{2,1,0:T(8,128)(2,1)}, u32[]{:S(2)}) copy-start(bf16[1,2048,768]{2,1,0:T(8,128)(2,1)} %param.14) | copy-start | bytes 9437188
  330.9 5.3 copy-start.4
  330.9 5.3 copy-start.5
Sparse Core Ops, SparseCore 0:
  341.1 223.0 reduce-scatter.1
